TPU v7x, 256 devices: a whole 4x4x8 slice. The times are simulated.
256 devices in a mesh: snap: 4 (over x), line: 64 (over z, y, core).
Axes of the slice: x: 4, y: 4, z: 8, core: 2. Of those that a mesh axis runs over, the one named last changes fastest.
Arguments:
- ptdf_rows: float32 [8192, 20480], P('line'), may hold values from -4 to 4
- plan: float32 [5120, 2048], P(('snap', 'line')), may hold values from 0 to 0.15
- unit_bus: int32 [5120], replicated, may hold values from 0 to 20479
- min_up: int32 [5120], P(('snap', 'line')), may hold values from 1 to 24, as said below
- ramp_lag: int32 [5120], P(('snap', 'line')), may hold values from 1 to 6, as said below
- load_share: float32 [20480], replicated, may hold values from 0.004 to 0.04
- system_load: float32 [2048], P('snap'), may hold values from 0.6 to 1.4
- corridor_order: int32 [4], replicated, may hold values from 0 to 3, each once
- corridor_buses: int32 [4, 2], replicated, may hold values from 0 to 20479, as said below
- corridor_owner: int32 [4], replicated, may hold values from 0 to 63
- corridor_row: int32 [4], replicated, may hold values from 0 to 127
- corridor_ratio: float32 [4], replicated, may hold values from 0.5 to 2
Outputs:
- flows: float32 [8192, 2048], P('line', 'snap')
- corridor_sens: float32 [4, 20480], replicated
Inputs may be any that keep to these rules, and one draw needn't show every extreme that they name: `min_up`: some unit has a window of exactly 24. `ramp_lag`: some unit has a lag of exactly 6. `corridor_buses`: the two buses of a corridor differ.
All inputs are finite; a program needn't handle non-finite values.
Results may differ from a plain program's by a relative error of at most 0.000098.
Values sent between devices are 32-bit elements; how exact they have to be, the bound alone decides.
No kernel may reach another device: no remote copies, remote signals or barrier semaphores. Data moves between devices by JAX's collectives and lax.ppermute only.
A program may use at most 128 MiB of HBM per device.

v0:
```python
import jax
import jax.numpy as jnp
from jax import lax
from jax.sharding import Mesh
from jax.sharding import PartitionSpec as P

WMAX = 24
NC = 4
LINE = ("line_0", "line_1", "line_2")
SNAP_LINE = ("snap", "line_0", "line_1", "line_2")
ramp_gain = 0.5


def in_blocks(x, dim, peers):
    before, after = (x.shape[:dim], x.shape[dim + 1 :])
    return jnp.moveaxis(x.reshape(*before, peers, -1, *after), dim, 0)


def sum_at_owner(x, axis, dim):
    tiles = in_blocks(x, dim, lax.axis_size(axis))
    arrived = lax.all_to_all(tiles, axis, split_axis=0, concat_axis=0, tiled=True)
    return arrived.sum(axis=0)


def summed_rows(x, axes, dim):
    far, near = axes
    tiles = in_blocks(x, dim, lax.axis_size(far))
    nearer = sum_at_owner(tiles, near, dim + 1)
    arrived = lax.all_to_all(nearer, far, split_axis=0, concat_axis=0, tiled=True)
    return arrived.sum(axis=0)


def padded_to(lines, peers):
    spare = -len(lines) % peers
    return jnp.pad(lines, [(0, spare)] + [(0, 0)] * (lines.ndim - 1))


def copy_for_each(x, axis):
    peers = lax.axis_size(axis)
    return lax.all_to_all(jnp.broadcast_to(x[None], (peers, *x.shape)), axis, 0, 0, tiled=True)


def joined_along(tiles, dim):
    lengths = list(tiles.shape[1:])
    lengths[dim] *= tiles.shape[0]
    return jnp.moveaxis(tiles, 0, dim).reshape(lengths)


def gathered_by_axis(x, axes, dim):
    far, near = axes
    leading = copy_for_each(x, far)
    tiles = jnp.swapaxes(copy_for_each(leading, near), 0, 1)
    return joined_along(tiles.reshape(-1, *x.shape), dim)


def total_of(x, axes):
    own = summed_rows(padded_to(x, lax.axis_size(axes[0]) * lax.axis_size(axes[1])), axes, 0)
    whole = gathered_by_axis(own, axes, 0)
    return whole[: len(x)].reshape(x.shape)


def together(arrays, axis):
    ends = [0]
    for a in arrays:
        ends.append(ends[-1] + a.size)
    subtotal = total_of(jnp.concatenate([a.ravel() for a in arrays]), axis)
    return tuple((subtotal[b:e].reshape(a.shape) for a, b, e in zip(arrays, ends, ends[1:])))


def body(
    ptdf_rows,
    plan,
    unit_bus,
    min_up,
    ramp_lag,
    load_share,
    system_load,
    corridor_order,
    corridor_buses,
    corridor_owner,
    corridor_row,
    corridor_ratio,
):
    unit_count, horizon = plan.shape
    snap_count = lax.axis_size("snap")
    line_count = lax.axis_size(LINE)
    padded = jnp.pad(plan, ((0, 0), (WMAX, 0)))
    inverse = 1.0 / min_up.astype(jnp.float32)
    held_mean = jnp.zeros(plan.shape, jnp.float32)
    lagged = jnp.zeros(plan.shape, jnp.float32)
    for offset in range(WMAX):
        shifted = padded[:, WMAX - offset : WMAX - offset + horizon]
        held_mean = held_mean + shifted * jnp.where(offset < min_up, inverse, 0.0)[:, None]
        lagged = lagged + shifted * (ramp_lag == offset).astype(jnp.float32)[:, None]
    dispatch = held_mean + ramp_gain * (plan - lagged)
    unit_blocks = lax.all_to_all(dispatch, "snap", split_axis=1, concat_axis=0, tiled=True)
    order_ids = unit_bus.reshape(snap_count, line_count, unit_count).transpose(1, 0, 2).reshape(-1)
    columns = jnp.take(ptdf_rows, order_ids, axis=1)
    gen_flows = jnp.dot(
        columns,
        lax.all_gather(unit_blocks, LINE, axis=0, tiled=True),
        preferred_element_type=jnp.float32,
        precision=lax.Precision.HIGHEST,
    )
    load_flows = jnp.dot(
        ptdf_rows, load_share, preferred_element_type=jnp.float32, precision=lax.Precision.HIGHEST
    )
    base = gen_flows - load_flows[:, None] * system_load[None, :]
    here = lax.axis_index(LINE)
    picked_rows = []
    picked_flows = []
    for step in range(NC):
        chosen = corridor_order[step]
        local_row = corridor_row[chosen]
        mine = corridor_owner[chosen] == here
        picked_rows.append(jnp.where(mine, ptdf_rows[local_row], 0.0))
        picked_flows.append(jnp.where(mine, base[local_row], 0.0))
    all_rows, all_flows = together(
        (jnp.stack(picked_rows), jnp.stack(picked_flows)), (("line_0", "line_1"), "line_2")
    )
    coeff_list = []
    sens_list = []
    shift_list = []
    ends_list = []
    for step in range(NC):
        chosen = corridor_order[step]
        bus_from = corridor_buses[chosen, 0]
        bus_to = corridor_buses[chosen, 1]
        ratio = corridor_ratio[chosen]
        coefficient = ptdf_rows[:, bus_from] - ptdf_rows[:, bus_to]
        for prior in range(step):
            coefficient = coefficient - coeff_list[prior] * (
                sens_list[prior][bus_from] - sens_list[prior][bus_to]
            )
        initial = all_rows[step]
        current = initial
        line_flow = all_flows[step]
        row_coeffs = []
        for prior in range(step):
            prior_from, prior_to = ends_list[prior]
            value = initial[prior_from] - initial[prior_to]
            for earlier in range(prior):
                value = value - row_coeffs[earlier] * (
                    sens_list[earlier][prior_from] - sens_list[earlier][prior_to]
                )
            row_coeffs.append(value)
        for prior in range(step):
            current = current - row_coeffs[prior] * sens_list[prior]
            line_flow = line_flow - row_coeffs[prior] * shift_list[prior]
        weight = ratio / (1.0 + ratio * jnp.abs(current[bus_from] - current[bus_to]))
        coeff_list.append(coefficient)
        sens_list.append(weight * current)
        shift_list.append(weight * line_flow)
        ends_list.append((bus_from, bus_to))
    flows = base
    for step in range(NC):
        flows = flows - coeff_list[step][:, None] * shift_list[step][None, :]
    return (flows, jnp.stack(sens_list))


def solution(mesh):
    torus = Mesh(
        mesh.devices.reshape(mesh.shape["snap"], 8, 4, 2), ("snap", "line_0", "line_1", "line_2")
    )
    in_specs = (
        P(LINE, None),
        P(SNAP_LINE, None),
        P(),
        P(SNAP_LINE),
        P(SNAP_LINE),
        P(),
        P("snap"),
        P(),
        P(),
        P(),
        P(),
        P(),
    )
    out_specs = (P(LINE, "snap"), P())
    return jax.shard_map(body, mesh=torus, in_specs=in_specs, out_specs=out_specs, check_vma=False)
```

profile of v0, /device:TPU:1, one launch (start us, length us, event | category | flops | bytes accessed | tf_op | source)
XLA Modules:
  0.0 217.8 jit_solution(7106054973172409046)
XLA Ops:
  7.2 0.7 compare_select_fusion.25
  9.3 6.7 %multiply_add_fusion = f32[20,2048]{1,0:T(8,128)S(1)} fusion(f32[20,2048]{1,0:T(8,128)} %param.13, f32[20]{0:T(128)S(1)} %get-tuple-element.133, f32[20]{0:T(128)S(1)} %get-tuple-element.134, f32[20]{0:T(128)S(1)} %get-tuple-element.112, f32[20]{0:T(128)S(1)} %get-tuple-element.113, f32[20]{0:T(128)S(1)} %get-tuple-element.114, ...), kind=kLoop, calls=%fused_computation.11 | loop fusion | flops 3973120 | bytes 331520 | tf_op jit(solution)/shard_map/add | solution.py:95
  16.2 9.8 %all_to_all.44 = f32[20,4,512]{2,0,1:T(8,128)S(1)} all-to-all(f32[20,4,512]{2,0,1:T(8,128)S(1)} %copy.27), channel_id=1, replica_groups=mesh['snap'=4,'line_0'=8,'line_1'=4,'line_2'=2] {'snap'}, dimensions={1} | all-to-all | bytes 327680 | tf_op jit(solution)/shard_map/all_to_all | solution.py:96
  26.0 0.7 all_to_all.33
  26.7 0.9 reshape.185
  28.0 1.4 fusion.31
  36.8 1.5 fusion.29
  43.4 11.8 %copy.26 = f32[128,20480]{0,1:T(8,128)} copy(f32[128,20480]{1,0:T(8,128)} %param.12) | data formatting | bytes 20971520 | tf_op args[0]
  60.3 2.0 broadcast_select_fusion.3
  62.7 17.4 %gather_fusion = f32[5120,128]{1,0:T(8,128)S(1)} fusion(f32[128,20480]{0,1:T(8,128)} %copy.26, s32[5120]{0:T(1024)S(1)} %broadcast_clamp_fusion), kind=kCustom, calls=%fused_computation | custom fusion | bytes 5263360 | tf_op jit(solution)/shard_map/jit(_take)/gather | solution.py:98
  80.1 10.9 %convolution_bitcast_fusion = f32[128]{0:T(128)S(1)} fusion(f32[128,20480]{1,0:T(8,128)} %param.12, f32[20480,1]{0,1:T(1,128)S(1)} %bitcast.64), kind=kOutput, calls=%fused_computation.6 | convolution fusion | flops 31457280 | bytes 10568192 | tf_op jit(solution)/shard_map/dot_general | solution.py:105
  91.0 24.8 %all-gather.2.cloned.1.call-done = f32[5120,512]{1,0:T(8,128)} async-done(((f32[80,512]{1,0:T(8,128)}), f32[5120,512]{1,0:T(8,128)}) %all-gather.2.cloned.1.call-update) | async-done | bytes 10485776 | tf_op jit(solution)/shard_map/all_gather | solution.py:101
  115.9 10.9 %fusion.4 = f32[128,512]{1,0:T(8,128)S(1)} fusion(f32[5120,512]{1,0:T(8,128)} %all-gather.2.cloned.1.call-done, f32[5120,128]{1,0:T(8,128)S(1)} %gather_fusion, pred[5120]{0:T(1024)(128)(4,1)S(1)} %compare_and_fusion, f32[512]{0:T(512)S(1)} %copy-done.3, f32[128]{0:T(128)S(1)} %convolution_bitcast_fusion), kind=kOutput, calls=%fused_computation.5 | convolution fusion | flops 4027318272 | bytes 13377024 | tf_op jit(solution)/shard_map/dot_general | solution.py:99
  127.3 3.9 %all_to_all.45 = f32[2,32,1312]{2,1,0:T(8,128)S(1)} all-to-all(f32[2,32,1312]{2,1,0:T(8,128)S(1)} %copy.28), channel_id=1, replica_groups=mesh['snap'=4,'line_0'=8,'line_1'=4,'line_2'=2] {'line_2'}, dimensions={0} | all-to-all | bytes 671744 | tf_op jit(solution)/shard_map/all_to_all | solution.py:21
  131.3 15.7 %all_to_all.46 = f32[32,1,1312]{2,1,0:T(1,128)S(1)} all-to-all(f32[32,1,1312]{2,1,0:T(1,128)S(1)} %all_to_all.35), channel_id=1, replica_groups=mesh['snap'=4,'line_0'=8,'line_1'=4,'line_2'=2] {'line_0','line_1'}, dimensions={0} | all-to-all | bytes 335872 | tf_op jit(solution)/shard_map/all_to_all | solution.py:29
  147.1 0.8 broadcast_in_dim.62
  147.9 4.0 %all-to-all-start.3 = ((f32[32,1,1312]{2,1,0:T(1,128)}), f32[32,1,1312]{2,1,0:T(1,128)S(1)}, u32[]{:S(2)}, u32[]{:S(2)}) async-start(f32[32,1,1312]{2,1,0:T(1,128)} %broadcast_in_dim.62), calls=%async_computation.3 | async-start | bytes 360448 | tf_op jit(solution)/shard_map/all_to_all | solution.py:40
  151.9 0.7 constant_dynamic-slice_fusion.8
  168.3 5.4 %all_to_all.47 = f32[2,32,1312]{2,1,0:T(8,128)S(1)} all-to-all(f32[2,32,1312]{2,1,0:T(8,128)S(1)} %broadcast_in_dim.64), channel_id=1, replica_groups=mesh['snap'=4,'line_0'=8,'line_1'=4,'line_2'=2] {'line_2'}, dimensions={0} | all-to-all | bytes 671744 | tf_op jit(solution)/shard_map/all_to_all | solution.py:40
  185.7 1.1 multiply_subtract_fusion.5
  192.5 0.7 fusion.19
  207.8 1.0 pad_maximum_fusion.1
  208.9 1.2 fusion.7
  210.1 0.9 multiply_subtract_fusion
  (52 shorter events, 10.4 us)
Async XLA Ops:
  7.2 72.9 %copy-start = (f32[20480]{0:T(1024)S(1)}, f32[20480]{0:T(1024)}, u32[]{:S(2)}) copy-start(f32[20480]{0:T(1024)} %param.17) | copy-start | bytes 245764
  7.2 108.7 %all-gather.2.cloned.1.call-start = ((), (), s32[]{:S(2)}) async-start(), calls=%async_computation.5 | async-start | bytes 10649600 | tf_op jit(solution)/shard_map/all_gather | solution.py:101
  80.1 35.8 %copy-start.3 = (f32[512]{0:T(512)S(1)}, f32[512]{0:T(512)}, u32[]{:S(2)}) copy-start(f32[512]{0:T(512)} %param.18) | copy-start | bytes 6148
  91.0 60.9 %copy-start.1 = (s32[4,2]{0,1:T(2,128)S(1)}, s32[4,2]{0,1:T(2,128)}, u32[]{:S(2)}) copy-start(s32[4,2]{0,1:T(2,128)} %param.20) | copy-start | bytes 100
  91.0 76.6 %copy-start.2 = (f32[4]{0:T(128)S(1)}, f32[4]{0:T(128)}, u32[]{:S(2)}) copy-start(f32[4]{0:T(128)} %param.23) | copy-start | bytes 52
  147.9 20.4 %all-to-all-start.3 = ((f32[32,1,1312]{2,1,0:T(1,128)}), f32[32,1,1312]{2,1,0:T(1,128)S(1)}, u32[]{:S(2)}, u32[]{:S(2)}) async-start(f32[32,1,1312]{2,1,0:T(1,128)} %broadcast_in_dim.62), calls=%async_computation.3 | async-start | bytes 360448 | tf_op jit(solution)/shard_map/all_to_all | solution.py:40
Sparse Core Ops, SparseCore 0:
  26.8 89.0 all-gather.1
where the time goes:
time: 219 us; the launch traced here: 218 us
  between operations  72.5 us (33%)
  local copies, waits for them, and re-layouts  44.2 us (20%)
  blocking collectives  34.8 us (16%)
  waiting for transfers between devices  24.8 us (11%)
  matrix products  21.8 us (10%)
  other arithmetic  15.6 us (7%)
  starting transfers between devices  4.03 us (2%)
    all_gather x1, waiting for transfers between devices, body(): lax.all_gather(unit_blocks, LINE, axis=0, tiled=True)  24.8 us
    gather x1, local copies, waits for them, and re-layouts, body(): columns = jnp.take(ptdf_rows, order_ids, axis=1)  17.4 us
    all_to_all x1, blocking collectives, summed_rows(): lax.all_to_all(nearer, far, split_axis=0, concat_axis=0, tiled=True)  15.7 us
    unnamed x12, local copies, waits for them, and re-layouts  11.9 us
    dot_general x1, matrix products, body(): jnp.dot(columns, lax.all_gather(unit_blocks, LINE, axis=0, tiled=True), p...  10.9 us
    dot_general x1, matrix products, body(): jnp.dot(ptdf_rows, load_share, preferred_element_type=jnp.float32, precis...  10.9 us
    all_to_all x1, blocking collectives, body(): lax.all_to_all(dispatch, 'snap', split_axis=1, concat_axis=0, tiled=True)  9.81 us
    add x1, other arithmetic, body(): dispatch = held_mean + ramp_gain * (plan - lagged)  6.69 us
  transfers between devices with their start and end apart: 2, of which 1 were waited for; matrix products, arithmetic and copies ran while one was open for 22% of the time, Pallas kernels for 0%

commit v1 on v0

--- a/solution.py
+++ b/solution.py
@@ -98,7 +98,9 @@
     columns = jnp.take(ptdf_rows, order_ids, axis=1)
     gen_flows = jnp.dot(
         columns,
-        lax.all_gather(unit_blocks, LINE, axis=0, tiled=True),
+        jnp.concatenate(
+            lax.all_to_all(jnp.stack([unit_blocks] * lax.axis_size(LINE), axis=0), LINE, 0, 0), 0
+        ),
         preferred_element_type=jnp.float32,
         precision=lax.Precision.HIGHEST,
     )

time: 219 us -> 367 us (1.68)
  waiting for transfers between devices: 24.8 us -> 166 us
  starting transfers between devices: 4.03 us -> 18.1 us
  between operations: 72.5 us -> 58.8 us
  blocking collectives: 34.8 us -> 39.5 us
    all_to_all x0 -> x1, waiting for transfers between devices: none -> 166 us  [body(): lax.all_to_all(jnp.stack([unit_blocks] * lax.axis_size(LINE), axis=0), LI...]
    all_gather x1 -> x0, waiting for transfers between devices: 24.8 us -> none  [body(): lax.all_gather(unit_blocks, LINE, axis=0, tiled=True)]
    all_to_all x0 -> x1, starting transfers between devices: none -> 14.1 us  [body(): lax.all_to_all(jnp.stack([unit_blocks] * lax.axis_size(LINE), axis=0), LI...]
    another operation x0 -> x2, local copies, waits for them, and re-layouts: none -> 5.19 us  [body(): jnp.stack([unit_blocks] * lax.axis_size(LINE), axis=0)]
    unnamed x12 -> x20, local copies, waits for them, and re-layouts: 11.9 us -> 11.8 us
  transfers between devices with their start and end apart: 2 -> 2, of which waited for: 1 -> 1; matrix products, arithmetic and copies ran while one was open for 22% -> 12% of each run, Pallas kernels for 0% -> 0%
where the time goes in v1:
time: 367 us; the launch traced here: 366 us
  waiting for transfers between devices  166 us (45%)
  between operations  58.8 us (16%)
  local copies, waits for them, and re-layouts  46.3 us (13%)
  blocking collectives  39.5 us (11%)
  matrix products  21.8 us (6%)
  starting transfers between devices  18.1 us (5%)
  other arithmetic  14.7 us (4%)
    all_to_all x1, waiting for transfers between devices, body(): lax.all_to_all(jnp.stack([unit_blocks] * lax.axis_size(LINE), axis=0), LI...  166 us
    gather x1, local copies, waits for them, and re-layouts, body(): columns = jnp.take(ptdf_rows, order_ids, axis=1)  17.4 us
    all_to_all x1, blocking collectives, summed_rows(): lax.all_to_all(nearer, far, split_axis=0, concat_axis=0, tiled=True)  17.3 us
    all_to_all x1, starting transfers between devices, body(): lax.all_to_all(jnp.stack([unit_blocks] * lax.axis_size(LINE), axis=0), LI...  14.1 us
    unnamed x20, local copies, waits for them, and re-layouts  11.8 us
    dot_general x1, matrix products, body(): jnp.dot(columns, jnp.concatenate(lax.all_to_all(jnp.stack([unit_blocks] *...  10.9 us
    dot_general x1, matrix products, body(): jnp.dot(ptdf_rows, load_share, preferred_element_type=jnp.float32, precis...  10.9 us
    all_to_all x1, blocking collectives, body(): lax.all_to_all(dispatch, 'snap', split_axis=1, concat_axis=0, tiled=True)  9.81 us
  transfers between devices with their start and end apart: 2, of which 1 were waited for; matrix products, arithmetic and copies ran while one was open for 12% of the time, Pallas kernels for 0%

profile of v1, /device:TPU:1, one launch (start us, length us, event | category | flops | bytes accessed | tf_op | source)
XLA Modules:
  0.0 365.6 jit_solution(16642601655106867987)
XLA Ops:
  0.6 0.7 compare_select_fusion.25
  2.7 5.9 %multiply_add_fusion = f32[20,2048]{1,0:T(8,128)S(1)} fusion(f32[20,2048]{1,0:T(8,128)} %param.13, f32[20]{0:T(128)S(1)} %get-tuple-element.133, f32[20]{0:T(128)S(1)} %get-tuple-element.134, f32[20]{0:T(128)S(1)} %get-tuple-element.112, f32[20]{0:T(128)S(1)} %get-tuple-element.113, f32[20]{0:T(128)S(1)} %get-tuple-element.114, ...), kind=kLoop, calls=%fused_computation.11 | loop fusion | flops 3973120 | bytes 331520 | tf_op jit(solution)/shard_map/add | solution.py:95
  8.8 9.8 %all_to_all.46 = f32[20,4,512]{2,0,1:T(8,128)S(1)} all-to-all(f32[20,4,512]{2,0,1:T(8,128)S(1)} %copy.27), channel_id=1, replica_groups=mesh['snap'=4,'line_0'=8,'line_1'=4,'line_2'=2] {'snap'}, dimensions={1} | all-to-all | bytes 327680 | tf_op jit(solution)/shard_map/all_to_all | solution.py:96
  18.6 5.2 %stack.19 = f32[64,80,512]{2,1,0:T(8,128)} broadcast(f32[80,512]{1,0:T(8,128)S(1)} %stack.18), dimensions={1,2} | broadcast | bytes 10649600 | tf_op jit(solution)/shard_map/stack | solution.py:102
  23.8 14.1 %all-to-all-start.1 = ((f32[64,80,512]{2,1,0:T(8,128)}), f32[64,80,512]{2,1,0:T(8,128)}, u32[]{:S(2)}, u32[]{:S(2)}) async-start(f32[64,80,512]{2,1,0:T(8,128)} %stack.19), calls=%async_computation.1 | async-start | bytes 20971520 | tf_op jit(solution)/shard_map/all_to_all | solution.py:102
  52.2 11.8 %copy.26 = f32[128,20480]{0,1:T(8,128)} copy(f32[128,20480]{1,0:T(8,128)} %param.12) | data formatting | bytes 20971520 | tf_op args[0]
  69.0 2.0 broadcast_select_fusion.3
  71.4 17.4 %gather_fusion = f32[5120,128]{1,0:T(8,128)S(1)} fusion(f32[128,20480]{0,1:T(8,128)} %copy.26, s32[5120]{0:T(1024)S(1)} %broadcast_clamp_fusion), kind=kCustom, calls=%fused_computation | custom fusion | bytes 5263360 | tf_op jit(solution)/shard_map/jit(_take)/gather | solution.py:98
  88.8 10.9 %convolution_bitcast_fusion = f32[128]{0:T(128)S(1)} fusion(f32[128,20480]{1,0:T(8,128)} %param.12, f32[20480,1]{0,1:T(1,128)S(1)} %bitcast.65), kind=kOutput, calls=%fused_computation.6 | convolution fusion | flops 31457280 | bytes 10568192 | tf_op jit(solution)/shard_map/dot_general | solution.py:107
  99.8 166.3 %all-to-all-done.1 = f32[64,80,512]{2,1,0:T(8,128)} async-done(((f32[64,80,512]{2,1,0:T(8,128)}), f32[64,80,512]{2,1,0:T(8,128)}, u32[]{:S(2)}, u32[]{:S(2)}) %all-to-all-start.1) | async-done | bytes 10485792 | tf_op jit(solution)/shard_map/all_to_all | solution.py:102
  266.1 10.9 %fusion.4 = f32[128,512]{1,0:T(8,128)S(1)} fusion(f32[5120,512]{1,0:T(8,128)} %bitcast.3, f32[5120,128]{1,0:T(8,128)S(1)} %gather_fusion, pred[5120]{0:T(1024)(128)(4,1)S(1)} %compare_and_fusion, f32[512]{0:T(512)S(1)} %copy-done.7, f32[128]{0:T(128)S(1)} %convolution_bitcast_fusion), kind=kOutput, calls=%fused_computation.5 | convolution fusion | flops 4027318272 | bytes 13377024 | tf_op jit(solution)/shard_map/dot_general | solution.py:99
  277.5 7.0 %all_to_all.47 = f32[2,32,1312]{2,1,0:T(8,128)S(1)} all-to-all(f32[2,32,1312]{2,1,0:T(8,128)S(1)} %copy.28), channel_id=1, replica_groups=mesh['snap'=4,'line_0'=8,'line_1'=4,'line_2'=2] {'line_2'}, dimensions={0} | all-to-all | bytes 671744 | tf_op jit(solution)/shard_map/all_to_all | solution.py:21
  284.7 17.3 %all_to_all.48 = f32[32,1,1312]{2,1,0:T(1,128)S(1)} all-to-all(f32[32,1,1312]{2,1,0:T(1,128)S(1)} %all_to_all.36), channel_id=1, replica_groups=mesh['snap'=4,'line_0'=8,'line_1'=4,'line_2'=2] {'line_0','line_1'}, dimensions={0} | all-to-all | bytes 335872 | tf_op jit(solution)/shard_map/all_to_all | solution.py:29
  302.1 0.8 broadcast_in_dim.62
  302.9 4.0 %all-to-all-start.4 = ((f32[32,1,1312]{2,1,0:T(1,128)}), f32[32,1,1312]{2,1,0:T(1,128)S(1)}, u32[]{:S(2)}, u32[]{:S(2)}) async-start(f32[32,1,1312]{2,1,0:T(1,128)} %broadcast_in_dim.62), calls=%async_computation.4 | async-start | bytes 360448 | tf_op jit(solution)/shard_map/all_to_all | solution.py:40
  306.9 0.7 constant_dynamic-slice_fusion.8
  323.2 5.4 %all_to_all.49 = f32[2,32,1312]{2,1,0:T(8,128)S(1)} all-to-all(f32[2,32,1312]{2,1,0:T(8,128)S(1)} %broadcast_in_dim.64), channel_id=1, replica_groups=mesh['snap'=4,'line_0'=8,'line_1'=4,'line_2'=2] {'line_2'}, dimensions={0} | all-to-all | bytes 671744 | tf_op jit(solution)/shard_map/all_to_all | solution.py:40
  337.6 0.7 fusion.23
  338.3 0.7 fusion.18
  340.3 1.1 multiply_subtract_fusion.5
  347.3 0.7 fusion.19
  362.5 1.0 pad_maximum_fusion.1
  363.6 1.2 fusion.7
  364.7 0.9 multiply_subtract_fusion
  (60 shorter events, 10.4 us)
Async XLA Ops:
  0.6 88.2 %copy-start = (f32[20480]{0:T(1024)S(1)}, f32[20480]{0:T(1024)}, u32[]{:S(2)}) copy-start(f32[20480]{0:T(1024)} %param.17) | copy-start | bytes 245764
  23.8 14.1 %copy-start.1 = (s32[5120]{0:T(1024)S(1)}, s32[5120]{0:T(1024)}, u32[]{:S(2)}) copy-start(s32[5120]{0:T(1024)} %param.14) | copy-start | bytes 61444
  23.8 14.7 %copy-start.6 = (s32[4]{0:T(128)S(1)}, s32[4]{0:T(128)}, u32[]{:S(2)}) copy-start(s32[4]{0:T(128)} %param.19) | copy-start | bytes 52
  23.8 22.7 %copy-start.3 = (s32[4]{0:T(128)S(1)}, s32[4]{0:T(128)}, u32[]{:S(2)}) copy-start(s32[4]{0:T(128)} %param.22) | copy-start | bytes 52
  23.8 22.7 %copy-start.4 = (s32[4]{0:T(128)S(1)}, s32[4]{0:T(128)}, u32[]{:S(2)}) copy-start(s32[4]{0:T(128)} %param.21) | copy-start | bytes 52
  23.8 242.3 %all-to-all-start.1 = ((f32[64,80,512]{2,1,0:T(8,128)}), f32[64,80,512]{2,1,0:T(8,128)}, u32[]{:S(2)}, u32[]{:S(2)}) async-start(f32[64,80,512]{2,1,0:T(8,128)} %stack.19), calls=%async_computation.1 | async-start | bytes 20971520 | tf_op jit(solution)/shard_map/all_to_all | solution.py:102
  88.8 177.3 %copy-start.7 = (f32[512]{0:T(512)S(1)}, f32[512]{0:T(512)}, u32[]{:S(2)}) copy-start(f32[512]{0:T(512)} %param.18) | copy-start | bytes 6148
  99.8 207.1 %copy-start.2 = (s32[4,2]{0,1:T(2,128)S(1)}, s32[4,2]{0,1:T(2,128)}, u32[]{:S(2)}) copy-start(s32[4,2]{0,1:T(2,128)} %param.20) | copy-start | bytes 100
  99.8 222.7 %copy-start.5 = (f32[4]{0:T(128)S(1)}, f32[4]{0:T(128)}, u32[]{:S(2)}) copy-start(f32[4]{0:T(128)} %param.23) | copy-start | bytes 52
  302.9 20.2 %all-to-all-start.4 = ((f32[32,1,1312]{2,1,0:T(1,128)}), f32[32,1,1312]{2,1,0:T(1,128)S(1)}, u32[]{:S(2)}, u32[]{:S(2)}) async-start(f32[32,1,1312]{2,1,0:T(1,128)} %broadcast_in_dim.62), calls=%async_computation.4 | async-start | bytes 360448 | tf_op jit(solution)/shard_map/all_to_all | solution.py:40
